TPU v7x, 512 devices: a whole 4x8x8 slice. The times are simulated.
512 devices in a mesh: dp: 128 (over y, z, core), owner: 4 (over x).
Axes of the slice: x: 4, y: 8, z: 8, core: 2. Of those that a mesh axis runs over, the one named last changes fastest.
Arguments:
- embeddings: bfloat16 [65536, 1024], P(('dp', 'owner')), may hold values from -120 to 120
- assignment: int32 [65536], P(('dp', 'owner')), may hold values from 0 to 8191, as said below
- pair_list: int32 [8192], replicated, may hold values from 0 to 8191, as said below
Outputs:
- best_similarity: float32 [65536], P(('dp', 'owner'))
Inputs may be any that keep to these rules, and one draw needn't show every extreme that they name: `assignment`: row r's cluster id is (t * n + o) * 16 + c, where n is the number of owner indices, o the owner index of the device holding row r, t an index of dp and c below 16. Among the rows of one device at most 2 share one t, and on every device exactly 2 rows share some t. pair_list[pair_list[k]] = k for every cluster k; cluster k = (t * n + o) * 16 + c and its partner have the same t and different owner indices o.
All inputs are finite; a program needn't handle non-finite values.
Results may differ from a plain program's by a relative error of at most 0.00053.
Values may be sent and summed in bfloat16 or wider, within the bound.
No kernel may reach another device: no remote copies, remote signals or barrier semaphores. Data moves between devices by JAX's collectives and lax.ppermute only.
A program may use at most 64 MiB of HBM per device.

v0:
```python
import jax
import jax.numpy as jnp
from jax import lax
from jax.sharding import PartitionSpec as P

CPD = 16


def shards(embeddings, assignment, pair_list):
    rows, width = embeddings.shape
    n_dp = lax.axis_size("dp")
    n_owner = lax.axis_size("owner")
    capacity = 2 * rows // n_dp
    slots = capacity * n_dp
    here_owner = lax.axis_index("owner")
    here_dp = lax.axis_index("dp")
    all_ids = lax.all_gather(assignment, ("dp", "owner"), axis=0, tiled=False)
    all_ids = all_ids.reshape(n_dp, n_owner, rows)
    values = embeddings.astype(jnp.float32)
    unit = (values * lax.rsqrt(jnp.sum(values * values, axis=1, keepdims=True) + 1e-06)).astype(
        jnp.bfloat16
    )
    target = assignment // (n_owner * CPD)
    onehot = (target[:, None] == jnp.arange(n_dp, dtype=jnp.int32)[None, :]).astype(jnp.int32)
    slot = jnp.sum(jnp.cumsum(onehot, axis=0) * onehot, axis=1) - 1
    position = target * capacity + slot
    first_id = (here_dp * n_owner + here_owner) * CPD
    partners_mine = lax.dynamic_slice_in_dim(pair_list, first_id, CPD)
    send_rows = jnp.zeros((slots, width), jnp.bfloat16).at[position].set(unit)
    got_rows = lax.all_to_all(
        send_rows.reshape(n_dp, capacity, width), "dp", split_axis=0, concat_axis=0, tiled=True
    )
    mine = got_rows.reshape(slots, width)
    rows_p = lax.all_gather(mine, "owner", axis=0, tiled=True)
    hit = all_ids // (n_owner * CPD) == here_dp
    rank = jnp.cumsum(hit.astype(jnp.int32), axis=2) - 1
    which = hit[:, :, :, None] & (
        rank[:, :, :, None] == jnp.arange(capacity, dtype=jnp.int32)[None, None, None, :]
    )
    filled = jnp.any(which, axis=2)
    table = jnp.sum(jnp.where(which, all_ids[:, :, :, None], 0), axis=2)
    table = jnp.where(filled, table, -1)
    ids_p = jnp.transpose(table, (1, 0, 2)).reshape(n_owner * slots)
    mine_ids = lax.dynamic_slice_in_dim(ids_p, here_owner * slots, slots)
    local = jnp.clip(mine_ids - first_id, 0, CPD - 1)
    picked = local[:, None] == jnp.arange(CPD, dtype=jnp.int32)[None, :]
    partner = jnp.sum(jnp.where(picked, partners_mine[None, :], 0), axis=1)
    scores = lax.dot_general(
        mine, rows_p, (((1,), (1,)), ((), ())), preferred_element_type=jnp.float32
    )
    column = jnp.arange(ids_p.shape[0], dtype=jnp.int32)
    itself = here_owner * slots + jnp.arange(slots, dtype=jnp.int32)
    same = (
        (mine_ids[:, None] == ids_p[None, :])
        & (ids_p[None, :] >= 0)
        & (itself[:, None] != column[None, :])
    )
    related = same | (partner[:, None] == ids_p[None, :])
    best = jnp.maximum(-1.0, jnp.max(jnp.where(related, scores, -1.0), axis=1))
    every_best = lax.all_gather(best, "dp", axis=0, tiled=True)
    back = target * slots + here_dp * capacity + slot
    return jnp.take(every_best, back)


def solution(mesh):
    placed = (P(("dp", "owner"), None), P(("dp", "owner")), P())
    return jax.shard_map(
        shards, mesh=mesh, in_specs=placed, out_specs=P(("dp", "owner")), check_vma=False
    )
```

profile of v0, /device:TPU:1, one launch (start us, length us, event | category | flops | bytes accessed | tf_op | source)
XLA Modules:
  0.0 210.9 jit_solution(3328990106305142735)
XLA Ops:
  6.5 0.0 all-gather.5.cloned.1.call-start
  6.5 0.7 and_select_fusion.1
  7.2 0.1 fusion.16
  7.3 0.2 reduce_window_sum.22
  7.5 0.2 select_reduce_fusion.1
  7.6 1.1 fusion.3
  8.7 0.7 compare_select_fusion.1
  9.4 0.0 copy-start.1
  9.4 1.8 scatter_custom_fusion
  11.2 0.2 reshape.108
  11.4 37.7 %all_to_all.5 = bf16[128,2,1024]{2,1,0:T(2,128)(2,1)S(1)} all-to-all(bf16[128,2,1024]{2,1,0:T(2,128)(2,1)S(1)} %reshape.108), channel_id=1, replica_groups=mesh['dp'=128,'owner'=4] {'dp'}, dimensions={0} | all-to-all | bytes 1048576 | tf_op jit(solution)/shard_map/all_to_all | solution.py:30
  49.1 1.0 reshape.109
  50.1 0.0 all-gather.5.cloned.1.call-update
  50.2 96.7 %all-gather.1 = s32[512,1,128]{2,1,0:T(1,128)S(1)} all-gather(s32[1,1,128]{2,1,0:T(1,128)S(1)} %bitcast.12), channel_id=2, replica_groups=mesh['dp'=128,'owner'=4] {'dp','owner'}, dimensions={0}, use_global_device_ids=true | all-gather | bytes 262656 | tf_op jit(solution)/shard_map/all_gather | solution.py:17
  146.8 0.2 copy.19
  147.0 0.4 fusion.8
  147.4 0.2 copy.23
  147.6 0.1 broadcast_add_fusion
  147.7 0.1 copy.24
  147.9 0.2 fusion.6
  148.1 0.2 select_reduce_fusion
  148.3 0.1 copy.26
  148.5 0.2 reshape.107
  148.7 0.8 dynamic_slice.7
  149.4 0.1 subtract_clamp_fusion
  149.5 0.1 select_reduce_fusion.2
  149.6 0.0 all-gather.5.cloned.1.call-done
  149.6 0.0 copy-done
  149.6 2.6 %fusion = f32[256]{0:T(256)S(1)} fusion(bf16[256,1024]{1,0:T(8,128)(2,1)S(1)} %copy-done, bf16[1024,1024]{1,0:T(8,128)(2,1)} %all-gather.5.cloned.1.call-done, s32[256]{0:T(256)S(1)} %get-tuple-element.9, s32[1024]{0:T(1024)S(1)} %reshape.107, s32[256]{0:T(256)S(1)} %select_reduce_fusion.2, s32[256]{0:T(256)S(1)} %get-tuple-element.6, ...), kind=kOutput, calls=%fused_computation.3 | convolution fusion | flops 538967808 | bytes 2630656 | tf_op jit(solution)/shard_map/dot_general | solution.py:48
  152.3 50.1 %all-gather.2 = f32[128,1,256]{2,1,0:T(1,128)S(1)} all-gather(f32[1,1,256]{2,1,0:T(1,128)S(1)} %bitcast.11), channel_id=1, replica_groups=mesh['dp'=128,'owner'=4] {'dp'}, dimensions={0}, use_global_device_ids=true | all-gather | bytes 132096 | tf_op jit(solution)/shard_map/all_gather | solution.py:60
  202.4 1.1 gather_fusion
  203.6 0.5 and_select_fusion
  (8 shorter events, 0.1 us)
Async XLA Ops:
  6.5 143.1 %all-gather.5.cloned.1.call-start = ((), (), s32[]{:S(2)}) async-start(), calls=%async_computation.1 | async-start | bytes 2621440 | tf_op jit(solution)/shard_map/all_gather | solution.py:34
  9.4 40.7 %copy-start.1 = (s32[128]{0:T(128)S(1)}, s32[128]{0:T(128)}, u32[]{:S(2)}) copy-start(s32[128]{0:T(128)} %param.4) | copy-start | bytes 1540
  50.1 99.5 %copy-start = (bf16[256,1024]{1,0:T(8,128)(2,1)S(1)}, bf16[256,1024]{1,0:T(8,128)(2,1)}, u32[]{:S(2)}) copy-start(bf16[256,1024]{1,0:T(8,128)(2,1)} %reshape.109) | copy-start | bytes 1572868
Sparse Core Ops, SparseCore 0:
  50.3 29.7 all-gather.4
where the time goes:
time: 211 us
  blocking collectives  184 us (87%)
  between operations  13.5 us (6%)
  other arithmetic  6.3 us (3%)
  local copies, waits for them, and re-layouts  3.92 us (2%)
  matrix products  2.64 us (1%)
    all_gather x1, blocking collectives, shards(): all_ids = lax.all_gather(assignment, ('dp', 'owner'), axis=0, tiled=False)  96.7 us
    all_gather x1, blocking collectives, shards(): every_best = lax.all_gather(best, 'dp', axis=0, tiled=True)  50.1 us
    all_to_all x1, blocking collectives, shards(): lax.all_to_all(send_rows.reshape(n_dp, capacity, width), 'dp', split_axis...  37.7 us
  transfers between devices with their start and end apart: 1, of which 0 were waited for; matrix products, arithmetic and copies ran while one was open for 1% of the time, Pallas kernels for 0%

commit v1 on v0

--- a/solution.py
+++ b/solution.py
@@ -57,7 +57,9 @@
     )
     related = same | (partner[:, None] == ids_p[None, :])
     best = jnp.maximum(-1.0, jnp.max(jnp.where(related, scores, -1.0), axis=1))
-    every_best = lax.all_gather(best, "dp", axis=0, tiled=True)
+    every_best = jnp.concatenate(
+        lax.all_to_all(jnp.stack([best] * lax.axis_size("dp")), "dp", 0, 0), axis=0
+    )
     back = target * slots + here_dp * capacity + slot
     return jnp.take(every_best, back)
 

time: 211 us -> 183 us (0.87)
  blocking collectives: 184 us -> 134 us
  waiting for transfers between devices: 0.03 us -> 12.2 us
  starting transfers between devices: 0.01 us -> 8.54 us
    all_gather x1 -> x0, blocking collectives: 50.1 us -> none  [shards(): every_best = lax.all_gather(best, 'dp', axis=0, tiled=True)]
    all_to_all x0 -> x1, waiting for transfers between devices: none -> 12.2 us  [shards(): lax.all_to_all(jnp.stack([best] * lax.axis_size('dp')), 'dp', 0, 0)]
    all_to_all x0 -> x1, starting transfers between devices: none -> 8.54 us  [shards(): lax.all_to_all(jnp.stack([best] * lax.axis_size('dp')), 'dp', 0, 0)]
  transfers between devices with their start and end apart: 1 -> 2, of which waited for: 0 -> 1; matrix products, arithmetic and copies ran while one was open for 1% -> 1% of each run, Pallas kernels for 0% -> 0%
where the time goes in v1:
time: 183 us; the launch traced here: 182 us
  blocking collectives  134 us (73%)
  between operations  13.6 us (7%)
  waiting for transfers between devices  12.2 us (7%)
  starting transfers between devices  8.54 us (5%)
  other arithmetic  6.3 us (3%)
  local copies, waits for them, and re-layouts  4.63 us (3%)
  matrix products  2.63 us (1%)
    all_gather x1, blocking collectives, shards(): all_ids = lax.all_gather(assignment, ('dp', 'owner'), axis=0, tiled=False)  96.7 us
    all_to_all x1, blocking collectives, shards(): lax.all_to_all(send_rows.reshape(n_dp, capacity, width), 'dp', split_axis...  37.7 us
    all_to_all x1, waiting for transfers between devices, shards(): lax.all_to_all(jnp.stack([best] * lax.axis_size('dp')), 'dp', 0, 0)  12.2 us
    all_to_all x1, starting transfers between devices, shards(): lax.all_to_all(jnp.stack([best] * lax.axis_size('dp')), 'dp', 0, 0)  8.54 us
  transfers between devices with their start and end apart: 2, of which 1 were waited for; matrix products, arithmetic and copies ran while one was open for 1% of the time, Pallas kernels for 0%

profile of v1, /device:TPU:1, one launch (start us, length us, event | category | flops | bytes accessed | tf_op | source)
XLA Modules:
  0.0 182.3 jit_solution(5512067182219593766)
XLA Ops:
  6.5 0.7 and_select_fusion.1
  7.2 0.1 fusion.16
  7.3 0.2 reduce_window_sum.22
  7.5 0.2 select_reduce_fusion.1
  7.6 1.1 fusion.3
  8.7 0.7 compare_select_fusion.1
  9.4 0.0 copy-start.1
  9.4 1.8 scatter_custom_fusion
  11.2 0.2 reshape.118
  11.4 37.7 %all_to_all.11 = bf16[128,2,1024]{2,1,0:T(2,128)(2,1)S(1)} all-to-all(bf16[128,2,1024]{2,1,0:T(2,128)(2,1)S(1)} %reshape.118), channel_id=1, replica_groups=mesh['dp'=128,'owner'=4] {'dp'}, dimensions={0} | all-to-all | bytes 1048576 | tf_op jit(solution)/shard_map/all_to_all | solution.py:30
  49.1 1.0 reshape.119
  50.1 0.0 all-gather.4.cloned.1.call-update
  50.2 96.7 %all-gather.1 = s32[512,1,128]{2,1,0:T(1,128)S(1)} all-gather(s32[1,1,128]{2,1,0:T(1,128)S(1)} %bitcast.10), channel_id=2, replica_groups=mesh['dp'=128,'owner'=4] {'dp','owner'}, dimensions={0}, use_global_device_ids=true | all-gather | bytes 262656 | tf_op jit(solution)/shard_map/all_gather | solution.py:17
  146.8 0.2 copy.19
  147.0 0.4 fusion.8
  147.4 0.2 copy.23
  147.6 0.1 broadcast_add_fusion
  147.7 0.1 copy.24
  147.9 0.2 fusion.6
  148.1 0.2 select_reduce_fusion
  148.3 0.1 copy.26
  148.5 0.2 reshape.117
  148.7 0.8 dynamic_slice.7
  149.4 0.1 subtract_clamp_fusion
  149.5 0.1 select_reduce_fusion.2
  149.6 0.0 all-gather.4.cloned.1.call-done
  149.6 2.6 %fusion = f32[256]{0:T(256)S(1)} fusion(bf16[256,1024]{1,0:T(8,128)(2,1)S(1)} %copy-done, bf16[1024,1024]{1,0:T(8,128)(2,1)} %all-gather.4.cloned.1.call-done, s32[256]{0:T(256)S(1)} %get-tuple-element.9, s32[1024]{0:T(1024)S(1)} %reshape.117, s32[256]{0:T(256)S(1)} %select_reduce_fusion.2, s32[256]{0:T(256)S(1)} %get-tuple-element.6, ...), kind=kOutput, calls=%fused_computation.3 | convolution fusion | flops 538967808 | bytes 2630656 | tf_op jit(solution)/shard_map/dot_general | solution.py:48
  152.3 0.7 stack.2
  153.0 8.5 %all-to-all-start.1 = ((f32[128,1,256]{2,1,0:T(1,128)}), f32[128,1,256]{2,1,0:T(1,128)S(1)}, u32[]{:S(2)}, u32[]{:S(2)}) async-start(f32[128,1,256]{2,1,0:T(1,128)} %stack.2), calls=%async_computation.1 | async-start | bytes 262144 | tf_op jit(solution)/shard_map/all_to_all | solution.py:61
  161.6 12.2 %all-to-all-done.1 = f32[128,1,256]{2,1,0:T(1,128)S(1)} async-done(((f32[128,1,256]{2,1,0:T(1,128)}), f32[128,1,256]{2,1,0:T(1,128)S(1)}, u32[]{:S(2)}, u32[]{:S(2)}) %all-to-all-start.1) | async-done | bytes 131104 | tf_op jit(solution)/shard_map/all_to_all | solution.py:61
  173.7 1.1 gather_fusion
  174.9 0.5 and_select_fusion
  (10 shorter events, 0.1 us)
Async XLA Ops:
  6.5 143.1 %all-gather.4.cloned.1.call-start = ((), (), s32[]{:S(2)}) async-start(), calls=%async_computation.2 | async-start | bytes 2621440 | tf_op jit(solution)/shard_map/all_gather | solution.py:34
  9.4 40.7 %copy-start.1 = (s32[128]{0:T(128)S(1)}, s32[128]{0:T(128)}, u32[]{:S(2)}) copy-start(s32[128]{0:T(128)} %param.4) | copy-start | bytes 1540
  50.1 99.5 %copy-start = (bf16[256,1024]{1,0:T(8,128)(2,1)S(1)}, bf16[256,1024]{1,0:T(8,128)(2,1)}, u32[]{:S(2)}) copy-start(bf16[256,1024]{1,0:T(8,128)(2,1)} %reshape.119) | copy-start | bytes 1572868
  153.0 20.8 %all-to-all-start.1 = ((f32[128,1,256]{2,1,0:T(1,128)}), f32[128,1,256]{2,1,0:T(1,128)S(1)}, u32[]{:S(2)}, u32[]{:S(2)}) async-start(f32[128,1,256]{2,1,0:T(1,128)} %stack.2), calls=%async_computation.1 | async-start | bytes 262144 | tf_op jit(solution)/shard_map/all_to_all | solution.py:61
Sparse Core Ops, SparseCore 0:
  50.3 29.7 all-gather.3
